TPU v7x, 128 devices: a whole 4x4x4 slice. The times are simulated.
128 devices in a mesh: group: 16 (over x, z), mp: 8 (over y, core).
Axes of the slice: x: 4, y: 4, z: 4, core: 2. Of those that a mesh axis runs over, the one named last changes fastest.
Arguments:
- stream: bfloat16 [8192, 3584], P('group', 'mp'), may hold values from -6 to 6
- prenorm_gain: float32 [3584], replicated, may hold values from 0.25 to 12
- query_weight: bfloat16 [3584, 4096], P(None, 'mp'), may hold values from -0.09375 to 0.09375
- key_weight: bfloat16 [3584, 2048], P(None, 'mp'), may hold values from -0.09375 to 0.09375
- value_weight: bfloat16 [3584, 2048], P(None, 'mp'), may hold values from -0.09375 to 0.09375
- output_weight: bfloat16 [4096, 3584], P('mp'), may hold values from -0.09375 to 0.09375
- adapter_down_rows: bfloat16 [64, 16, 3584], P('group', None, 'mp'), may hold values from -0.09375 to 0.09375
- adapter_up_query: bfloat16 [64, 16, 4096], P('group', None, 'mp'), may hold values from -1.5 to 1.5
- request_adapter: int32 [16, 4], replicated, may hold values from 0 to 63
- adapter_row_index: int32 [64], replicated, may hold values from 0 to 63, each once
- request_token_length: int32 [16, 4], replicated, may hold values from 1 to 256, 512 in all within a row
- continues_previous: int32 [16], replicated, may hold values from 0 to 1, as said below
- request_cache_block: int32 [16, 4], replicated, may hold values from 0 to 31, as said below
- cached_length: int32 [16, 4], replicated, may hold values from 1 to 256
- cached_rotated_keys: bfloat16 [32, 256, 2048], P('group', None, 'mp'), may hold values from -6 to 6
- cached_value_rows: bfloat16 [32, 256, 2048], P('group', None, 'mp'), may hold values from -6 to 6
Outputs:
- attn_out: bfloat16 [8192, 3584], P('group', 'mp')
Inputs may be any that keep to these rules, and one draw needn't show every extreme that they name: `continues_previous`: the first group has 0; some group has 1. `request_cache_block`: the owner of block b is group b // 2; blocks may be shared by requests.
All inputs are finite; a program needn't handle non-finite values.
Results may differ from a plain program's by a relative error of at most 0.017.
The roundings to bfloat16 on the way count: a program that leaves them out, or rounds other values in their place, can miss the bound.
Values may be sent and summed in bfloat16 or wider, within the bound.
No kernel may reach another device: no remote copies, remote signals or barrier semaphores. Data moves between devices by JAX's collectives and lax.ppermute only.
A program may use at most 128 MiB of HBM per device.

v0:
```python
import jax
import jax.numpy as jnp
from jax import lax
from jax.sharding import PartitionSpec as P

HEAD_WIDTH = 256
REQS = 4
adapter_scale = 2.0


def shifted(value, axis, steps):
    count = lax.axis_size(axis)
    first, last = (max(0, -steps), min(count, count - steps))
    return lax.ppermute(value, axis, [(source, source + steps) for source in range(first, last)])


def rotate(values, position, head_size):
    count = values.shape[0]
    shaped = values.reshape(count, -1, head_size)
    half = head_size // 2
    freq = 10000.0 ** (-jnp.arange(half, dtype=jnp.float32) / half)
    angle = position[:, None, None] * freq[None, None, :]
    cosine = jnp.cos(angle)
    sine = jnp.sin(angle)
    first = shaped[..., :half]
    second = shaped[..., half:]
    turned = jnp.concatenate(
        [first * cosine - second * sine, second * cosine + first * sine], axis=-1
    )
    return turned.reshape(count, -1)


def layout(lengths, cached, split_flag, prev_len, count):
    ends = jnp.cumsum(lengths)
    starts = ends - lengths
    place = jnp.arange(count, dtype=jnp.int32)
    member = ((place[:, None] >= starts[None, :]) & (place[:, None] < ends[None, :])).astype(
        jnp.int32
    )
    request = jnp.sum(member * jnp.arange(lengths.shape[0], dtype=jnp.int32)[None, :], axis=1)
    offset = place - jnp.sum(member * starts[None, :], axis=1)
    extra = jnp.where(request == 0, split_flag * prev_len, 0)
    position = jnp.sum(member * cached[None, :], axis=1) + extra + offset
    return (member, request, position.astype(jnp.float32))


def attend(
    query_vectors,
    keys,
    values,
    prev_keys,
    prev_values,
    cache_keys,
    cache_values,
    request,
    cached,
    split_flag,
    prev_len,
    head_size,
):
    count = query_vectors.shape[0]
    kv_heads = keys.shape[1] // head_size
    ratio = query_vectors.shape[1] // keys.shape[1]
    block = cache_keys.shape[1]
    slots = cache_keys.shape[0] * block
    every_key = jnp.concatenate([cache_keys.reshape(slots, -1), prev_keys, keys], 0).reshape(
        -1, kv_heads, head_size
    )
    every_value = jnp.concatenate(
        [cache_values.reshape(slots, -1), prev_values, values], 0
    ).reshape(-1, kv_heads, head_size)
    slot_req = jnp.arange(slots, dtype=jnp.int32) // block
    slot_col = jnp.arange(slots, dtype=jnp.int32) % block
    cache_ok = (request[:, None] == slot_req[None, :]) & (
        slot_col[None, :] < cached[slot_req][None, :]
    )
    place = jnp.arange(count, dtype=jnp.int32)
    prev_ok = (split_flag == 1) & (request[:, None] == 0) & (place[None, :] >= count - prev_len)
    own_ok = (request[:, None] == request[None, :]) & (place[None, :] <= place[:, None])
    allowed = jnp.concatenate([cache_ok, prev_ok, own_ok], 1)
    grouped = query_vectors.reshape(count, kv_heads, ratio, head_size)
    scores = jnp.einsum(
        "tkrd,skd->krts", grouped, every_key, preferred_element_type=jnp.float32
    ) * head_size ** (-0.5)
    scores = jnp.where(allowed[None, None], scores, jnp.float32(-1e30))
    top = jnp.max(scores, axis=-1, keepdims=True)
    weights = jnp.exp(scores - top)
    total = jnp.sum(weights, axis=-1)
    numer = jnp.einsum(
        "krts,skd->tkrd",
        weights.astype(jnp.bfloat16),
        every_value,
        preferred_element_type=jnp.float32,
    )
    result = numer / jnp.transpose(total, (2, 0, 1))[..., None]
    return result.reshape(count, -1).astype(jnp.bfloat16)


def on_device(
    stream,
    prenorm_gain,
    query_weight,
    key_weight,
    value_weight,
    output_weight,
    adapter_down_rows,
    adapter_up_query,
    request_adapter,
    adapter_row_index,
    request_token_length,
    continues_previous,
    request_cache_block,
    cached_length,
    cached_rotated_keys,
    cached_value_rows,
):
    count = stream.shape[0]
    width = stream.shape[1]
    group_at = lax.axis_index("group")
    model_at = lax.axis_index("mp")
    whole = lax.all_gather(stream, "mp", axis=1, tiled=True)
    wide = whole.astype(jnp.float32)
    normalized_input = (
        wide * lax.rsqrt(jnp.mean(wide * wide, axis=1, keepdims=True) + 1e-06) * prenorm_gain
    ).astype(jnp.bfloat16)
    normed_part = lax.dynamic_slice_in_dim(normalized_input, model_at * width, width, 1)
    before = jnp.maximum(group_at - 1, 0)
    lengths = request_token_length[group_at]
    cached = cached_length[group_at]
    split_flag = continues_previous[group_at]
    prev_len = request_token_length[before, REQS - 1]
    member, request, position = layout(lengths, cached, split_flag, prev_len, count)
    wanted = adapter_row_index[request_adapter[group_at]]
    pieces = (
        lax.all_gather(adapter_down_rows, "group", axis=0, tiled=True),
        lax.all_gather(adapter_up_query, "group", axis=0, tiled=True),
    )
    stored = jnp.arange(pieces[0].shape[0], dtype=jnp.int32)
    onehot = (wanted[:, None] == stored[None, :]).astype(jnp.bfloat16)
    new_down = jnp.einsum("rj,jkd->rkd", onehot, pieces[0], preferred_element_type=jnp.float32)
    new_up = jnp.einsum("rj,jkd->rkd", onehot, pieces[1], preferred_element_type=jnp.float32)
    chosen_down = new_down.astype(jnp.bfloat16)
    chosen_up = new_up.astype(jnp.bfloat16)
    rank_index = adapter_down_rows.shape[1]
    partial_low = jnp.einsum(
        "td,rkd->trk", normed_part, chosen_down, preferred_element_type=jnp.float32
    ).reshape(count, REQS * rank_index)
    low = lax.psum(partial_low, "mp").astype(jnp.bfloat16)
    own_columns = jnp.repeat(member, rank_index, axis=1).astype(jnp.bfloat16)
    query_update = jnp.dot(
        low * own_columns,
        chosen_up.reshape(REQS * rank_index, -1),
        preferred_element_type=jnp.float32,
    )
    query_vectors = (
        jnp.dot(normalized_input, query_weight, preferred_element_type=jnp.float32)
        + adapter_scale * query_update
    )
    query_vectors = rotate(query_vectors, position, HEAD_WIDTH).astype(jnp.bfloat16)
    keys = rotate(
        jnp.dot(normalized_input, key_weight, preferred_element_type=jnp.float32),
        position,
        HEAD_WIDTH,
    ).astype(jnp.bfloat16)
    values = jnp.dot(normalized_input, value_weight, preferred_element_type=jnp.float32).astype(
        jnp.bfloat16
    )
    prev_keys, prev_values = shifted((keys, values), "group", 1)
    blocks = request_cache_block[group_at]
    pieces = (
        lax.all_gather(cached_rotated_keys, "group", axis=0, tiled=True),
        lax.all_gather(cached_value_rows, "group", axis=0, tiled=True),
    )
    stored = jnp.arange(pieces[0].shape[0], dtype=jnp.int32)
    onehot = (blocks[:, None] == stored[None, :]).astype(jnp.bfloat16)
    new_keys = jnp.einsum("rj,jcd->rcd", onehot, pieces[0], preferred_element_type=jnp.float32)
    new_values = jnp.einsum("rj,jcd->rcd", onehot, pieces[1], preferred_element_type=jnp.float32)
    cache_keys = new_keys.astype(jnp.bfloat16)
    cache_values = new_values.astype(jnp.bfloat16)
    attended = attend(
        query_vectors,
        keys,
        values,
        prev_keys,
        prev_values,
        cache_keys,
        cache_values,
        request,
        cached,
        split_flag,
        prev_len,
        HEAD_WIDTH,
    )
    partial_out = jnp.dot(attended, output_weight, preferred_element_type=jnp.float32)
    return lax.psum_scatter(partial_out.astype(jnp.bfloat16), "mp", scatter_dimension=1, tiled=True)


def solution(mesh):
    placed = (
        P("group", "mp"),
        P(),
        P(None, "mp"),
        P(None, "mp"),
        P(None, "mp"),
        P("mp", None),
        P("group", None, "mp"),
        P("group", None, "mp"),
        P(),
        P(),
        P(),
        P(),
        P(),
        P(),
        P("group", None, "mp"),
        P("group", None, "mp"),
    )
    return jax.shard_map(
        on_device, mesh=mesh, in_specs=placed, out_specs=P("group", "mp"), check_vma=False
    )
```

profile of v0, /device:TPU:0, one launch (start us, length us, event | category | flops | bytes accessed | tf_op | source)
XLA Modules:
  0.0 254.0 jit_solution(16617972660007501374)
XLA Ops:
  13.4 26.9 %all_gather.18 = bf16[64,16,448]{2,1,0:T(8,128)(2,1)S(1)} all-gather(bf16[4,16,448]{2,1,0:T(8,128)(2,1)} %param.22), channel_id=1, replica_groups=mesh['group'=16,'mp'=8] {'group'}, dimensions={0}, use_global_device_ids=true | all-gather | bytes 974848 | tf_op jit(solution)/shard_map/all_gather | solution.py:135
  40.9 2.6 %compare_select_fusion.1 = s32[1024,1]{0,1:T(1,128)S(1)} fusion(s32[]{:T(128)} %bitcast.7, s32[]{:T(128)} %bitcast.8, s32[]{:T(128)} %bitcast.10, s32[]{:T(128)} %bitcast.9), kind=kLoop, calls=%fused_computation.71 | loop fusion | flops 17408 | bytes 4112 | tf_op jit(solution)/shard_map/gather | solution.py:75
  49.5 1.8 multiply_cosine_fusion
  54.9 2.4 convolution_convert_fusion.2
  57.4 28.5 %all-gather.7.cloned.1.call-done = bf16[512,3584]{0,1:T(8,128)(2,1)} async-done(((bf16[512,448]{0,1:T(8,128)(2,1)}), bf16[512,3584]{0,1:T(8,128)(2,1)}) %all-gather.7.cloned.1.call-update) | async-done | bytes 3670032 | tf_op jit(solution)/shard_map/all_gather | solution.py:121
  85.8 3.0 %fusion.2 = f32[512]{0:T(512)S(1)} fusion(bf16[512,3584]{0,1:T(8,128)(2,1)} %all-gather.7.cloned.1.call-done), kind=kLoop, calls=%fused_computation.7 | loop fusion | flops 5504512 | bytes 3672064 | tf_op jit(solution)/shard_map/reduce_sum | solution.py:124
  90.6 1.8 copy-done.2
  92.4 1.9 convolution_convert_fusion.1
  96.1 4.2 %collective-permute-start = (bf16[512,256]{1,0:T(8,128)(2,1)}, bf16[512,256]{1,0:T(8,128)(2,1)}, u32[]{:S(2)}, u32[]{:S(2)}) collective-permute-start(bf16[512,256]{1,0:T(8,128)(2,1)} %convolution_convert_fusion.1), channel_id=1, source_target_pairs={{0,8},{8,16},{16,24},{24,32},{32,40},{40,48},{48,56},{56,64},{64,7... | collective-permute-start | bytes 786440 | tf_op jit(solution)/shard_map/ppermute | solution.py:14
  100.2 3.8 %convolution_bitcast_fusion = f32[512,1,256]{0,2,1:T(8,128)S(1)} fusion(bf16[512,3584]{0,1:T(8,128)(2,1)} %copy-done.2, bf16[3584,256]{1,0:T(8,128)(2,1)} %param.19), kind=kOutput, calls=%fused_computation.26 | convolution fusion | flops 939524096 | bytes 6029312 | tf_op jit(solution)/shard_map/dot_general | solution.py:161
  107.7 3.4 %collective-permute-start.1 = (bf16[512,256]{0,1:T(8,128)(2,1)}, bf16[512,256]{0,1:T(8,128)(2,1)}, u32[]{:S(2)}, u32[]{:S(2)}) collective-permute-start(bf16[512,256]{0,1:T(8,128)(2,1)} %maximum_bitcast_fusion.6), channel_id=1, source_target_pairs={{0,8},{8,16},{16,24},{24,32},{32,40},{40,48},{48,56},{56,64},{64,7... | collective-permute-start | bytes 786440 | tf_op jit(solution)/shard_map/ppermute | solution.py:14
  112.3 26.0 %all-reduce.1 = bf16[512,64]{0,1:T(8,128)(2,1)S(1)} all-reduce(f32[512,64]{0,1:T(8,128)S(1)} %bitcast.101), channel_id=1, replica_groups=mesh['group'=16,'mp'=8] {'mp'}, use_global_device_ids=true, to_apply=%region_5.6 | all-reduce | flops 32768 | bytes 196608 | tf_op jit(solution)/shard_map/psum | solution.py:148
  138.4 5.3 %fusion.82 = f32[512,512]{0,1:T(8,128)S(1)} fusion(bf16[512,3584]{0,1:T(8,128)(2,1)} %copy-done.2, bf16[3584,512]{1,0:T(8,128)(2,1)} %param.18), kind=kOutput, calls=%fused_computation.129 | convolution fusion | flops 1879048192 | bytes 8388608 | tf_op jit(solution)/shard_map/dot_general | solution.py:156
  146.4 2.1 copy.62
  148.5 2.2 subtract_convert_fusion
  150.6 1.8 copy.46
  154.3 4.6 %fusion.18 = bf16[4,256,256]{2,0,1:T(4,128)(2,1)S(1)} fusion(bf16[32,256,256]{2,1,0:T(8,128)(2,1)} %all-gather.5.cloned.1.call-done, s32[4]{0:T(128)S(1)} %dynamic-slice_reduce_fusion.1), kind=kOutput, calls=%fused_computation.24 | convolution fusion | flops 17039488 | bytes 4718608 | tf_op jit(solution)/shard_map/rj,jcd->rcd/dot_general | solution.py:177
  160.0 35.3 %all-gather.9.cloned.1.call-done = bf16[32,256,256]{2,1,0:T(8,128)(2,1)} async-done(((bf16[2,256,256]{2,1,0:T(8,128)(2,1)}), bf16[32,256,256]{2,1,0:T(8,128)(2,1)}) %all-gather.9.cloned.1.call-update) | async-done | bytes 4194320 | tf_op jit(solution)/shard_map/all_gather | solution.py:171
  195.3 4.7 %fusion.21 = bf16[4,256,256]{2,0,1:T(4,128)(2,1)S(1)} fusion(bf16[32,256,256]{2,1,0:T(8,128)(2,1)} %all-gather.9.cloned.1.call-done, s32[4]{0:T(128)S(1)} %dynamic-slice_reduce_fusion.1), kind=kOutput, calls=%fused_computation.25 | convolution fusion | flops 17039488 | bytes 4718608 | tf_op jit(solution)/shard_map/rj,jcd->rcd/dot_general | solution.py:176
  200.1 1.8 fusion.5
  201.9 2.2 fusion
  204.2 2.8 %divide_convert_fusion = bf16[512,1,2,256]{0,3,2,1:T(8,128)(2,1)S(1)} fusion(f32[2048,512,2]{1,0,2:T(8,128)S(1)} %get-tuple-element.25, f32[2,512]{1,0:T(2,128)S(1)} %get-tuple-element.24, pred[512,2048]{0,1:T(8,128)(4,1)S(1)} %pad_add_fusion, bf16[512,256]{0,1:T(8,128)(2,1)S(1)} %copy-done.4, bf16[512,256]{0,1:T(8,128)(2,1)S(1)} %copy-done.6, ...), kind=kOutput, calls=%fused_computation.43 | convolution fusion | flops 1085800448 | bytes 11018240 | tf_op jit(solution)/shard_map/krts,skd->tkrd/dot_general | solution.py:89
  207.0 3.9 %convolution_convert_fusion = bf16[512,3584]{0,1:T(8,128)(2,1)} fusion(bf16[512,512]{0,1:T(8,128)(2,1)S(1)} %bitcast.107, bf16[512,3584]{1,0:T(8,128)(2,1)S(1)} %copy-done.11), kind=kOutput, calls=%fused_computation.11 | convolution fusion | flops 1880883200 | bytes 7864320 | tf_op jit(solution)/shard_map/dot_general | solution.py:194
  210.9 36.5 %reduce-scatter.2.cloned.1.call-done = bf16[512,448]{0,1:T(8,128)(2,1)} async-done(((bf16[512,3584]{0,1:T(8,128)(2,1)}), bf16[512,448]{0,1:T(8,128)(2,1)}) %reduce-scatter.2.cloned.1.call-update) | async-done | bytes 458768 | tf_op jit(solution)/shard_map/reduce_scatter | solution.py:195
  (78 shorter events, 28.4 us)
Async XLA Ops:
  6.5 85.8 %copy-start = (bf16[3584,256]{1,0:T(8,128)(2,1)S(1)}, bf16[3584,256]{1,0:T(8,128)(2,1)}, u32[]{:S(2)}) copy-start(bf16[3584,256]{1,0:T(8,128)(2,1)} %param.20) | copy-start | bytes 5505028
  6.5 48.4 %all-gather.11.cloned.1.call-start = ((), (), s32[]{:S(2)}) async-start(), calls=%async_computation.4 | async-start | bytes 1114112 | tf_op jit(solution)/shard_map/all_gather | solution.py:136
  7.3 78.6 %all-gather.7.cloned.1.call-start = ((), (), s32[]{:S(2)}) async-start(), calls=%async_computation.2 | async-start | bytes 4128768 | tf_op jit(solution)/shard_map/all_gather | solution.py:121
  8.0 146.3 %all-gather.5.cloned.1.call-start = ((), (), s32[]{:S(2)}) async-start(), calls=%async_computation.1 | async-start | bytes 4456448 | tf_op jit(solution)/shard_map/all_gather | solution.py:172
  8.7 186.5 %all-gather.9.cloned.1.call-start = ((), (), s32[]{:S(2)}) async-start(), calls=%async_computation.3 | async-start | bytes 4456448 | tf_op jit(solution)/shard_map/all_gather | solution.py:171
  9.3 238.1 %reduce-scatter.2.cloned.1.call-start = ((), (), s32[]{:S(2)}) async-start(), calls=%async_computation.5 | async-start | bytes 4128768 | tf_op jit(solution)/shard_map/reduce_scatter | solution.py:195
  53.4 35.5 %copy-start.10 = (f32[3584]{0:T(1024)S(1)}, f32[3584]{0:T(1024)}, u32[]{:S(2)}) copy-start(f32[3584]{0:T(1024)} %param.17) | copy-start | bytes 43012
  85.8 3.1 %copy-start.1 = (bf16[512,3584]{0,1:T(8,128)(2,1)S(1)}, bf16[512,3584]{0,1:T(8,128)(2,1)}, u32[]{:S(2)}) copy-start(bf16[512,3584]{0,1:T(8,128)(2,1)} %all-gather.7.cloned.1.call-done) | copy-start | bytes 11010052
  90.5 1.8 copy-start.2
  96.1 54.6 %collective-permute-start = (bf16[512,256]{1,0:T(8,128)(2,1)}, bf16[512,256]{1,0:T(8,128)(2,1)}, u32[]{:S(2)}, u32[]{:S(2)}) collective-permute-start(bf16[512,256]{1,0:T(8,128)(2,1)} %convolution_convert_fusion.1), channel_id=1, source_target_pairs={{0,8},{8,16},{16,24},{24,32},{32,40},{40,48},{48,56},{56,64},{64,7... | collective-permute-start | bytes 786440 | tf_op jit(solution)/shard_map/ppermute | solution.py:14
  107.7 44.8 %collective-permute-start.1 = (bf16[512,256]{0,1:T(8,128)(2,1)}, bf16[512,256]{0,1:T(8,128)(2,1)}, u32[]{:S(2)}, u32[]{:S(2)}) collective-permute-start(bf16[512,256]{0,1:T(8,128)(2,1)} %maximum_bitcast_fusion.6), channel_id=1, source_target_pairs={{0,8},{8,16},{16,24},{24,32},{32,40},{40,48},{48,56},{56,64},{64,7... | collective-permute-start | bytes 786440 | tf_op jit(solution)/shard_map/ppermute | solution.py:14
  160.0 40.1 %copy-start.5 = (bf16[512,256]{1,0:T(8,128)(2,1)S(1)}, bf16[512,256]{1,0:T(8,128)(2,1)}, u32[]{:S(2)}) copy-start(bf16[512,256]{1,0:T(8,128)(2,1)} %copy.52) | copy-start | bytes 786436
  160.0 40.1 %copy-start.7 = (bf16[512,256]{1,0:T(8,128)(2,1)S(1)}, bf16[512,256]{1,0:T(8,128)(2,1)}, u32[]{:S(2)}) copy-start(bf16[512,256]{1,0:T(8,128)(2,1)} %copy.51) | copy-start | bytes 786436
  195.3 4.8 %copy-start.8 = (bf16[512,2,128]{2,0,1:T(8,128)(2,1)S(1)}, bf16[512,2,128]{2,0,1:T(8,128)(2,1)}, u32[]{:S(2)}) copy-start(bf16[512,2,128]{2,0,1:T(8,128)(2,1)} %get-tuple-element.12) | copy-start | bytes 786436
  195.3 4.8 %copy-start.9 = (bf16[512,2,128]{2,0,1:T(8,128)(2,1)S(1)}, bf16[512,2,128]{2,0,1:T(8,128)(2,1)}, u32[]{:S(2)}) copy-start(bf16[512,2,128]{2,0,1:T(8,128)(2,1)} %get-tuple-element.13) | copy-start | bytes 786436
  201.9 2.2 copy-start.3
  201.9 2.2 copy-start.4
  201.9 2.2 copy-start.6
  204.2 2.8 %copy-start.11 = (bf16[512,3584]{1,0:T(8,128)(2,1)S(1)}, bf16[512,3584]{1,0:T(8,128)(2,1)}, u32[]{:S(2)}) copy-start(bf16[512,3584]{1,0:T(8,128)(2,1)} %param.21) | copy-start | bytes 11010052
Sparse Core Ops, SparseCore 0:
  9.5 45.3 all-gather.10
  56.6 29.1 all-gather.6
  88.0 53.9 all-gather.4
  144.0 51.2 all-gather.8
  211.0 36.3 reduce-scatter.1
where the time goes:
time: 255 us; the launch traced here: 254 us
  waiting for transfers between devices  104 us (41%)
  blocking collectives  52.9 us (21%)
  matrix products  33.9 us (13%)
  local copies, waits for them, and re-layouts  21.9 us (9%)
  other arithmetic  17.3 us (7%)
  between operations  16.1 us (6%)
  starting transfers between devices  7.77 us (3%)
    reduce_scatter x1, waiting for transfers between devices, on_device(): lax.psum_scatter(partial_out.astype(jnp.bfloat16), 'mp', scatter_dimensio...  36.5 us
    all_gather x1, waiting for transfers between devices, on_device(): lax.all_gather(cached_rotated_keys, 'group', axis=0, tiled=True)  35.3 us
    all_gather x1, waiting for transfers between devices, on_device(): whole = lax.all_gather(stream, 'mp', axis=1, tiled=True)  28.5 us
    all_gather x1, blocking collectives, on_device(): lax.all_gather(adapter_down_rows, 'group', axis=0, tiled=True)  26.9 us
    psum x1, blocking collectives, on_device(): low = lax.psum(partial_low, 'mp').astype(jnp.bfloat16)  26 us
    ppermute x2, starting transfers between devices, shifted(): lax.ppermute(value, axis, [(source, source + steps) for source in range(f...  7.62 us
    unnamed x27, local copies, waits for them, and re-layouts  5.37 us
    dot_general x1, matrix products, on_device(): jnp.dot(normalized_input, query_weight, preferred_element_type=jnp.float32)  5.26 us
  transfers between devices with their start and end apart: 7, of which 4 were waited for; matrix products, arithmetic and copies ran while one was open for 22% of the time, Pallas kernels for 0%

commit v1 on v0

--- a/solution.py
+++ b/solution.py
@@ -1,3 +1,4 @@
+import functools
 import jax
 import jax.numpy as jnp
 from jax import lax
@@ -6,6 +7,36 @@
 HEAD_WIDTH = 256
 REQS = 4
 adapter_scale = 2.0
+
+
+def trace_the_body(mat, dim_i):
+    mat = jnp.moveaxis(mat, 0, dim_i)
+    far_arr = mat.shape
+    return mat.reshape(*far_arr[:dim_i], far_arr[dim_i] * far_arr[dim_i + 1], *far_arr[dim_i + 2 :])
+
+
+def _perform_panels(x0, axis_name, dim_at):
+    size_here = jax.lax.axis_size(axis_name)
+    arrivals = tuple(((j, (j + 1) % size_here) for j in range(size_here)))
+    ledger = tuple(((no, to_i) for to_i, no in arrivals))
+    then, raw_out = ([], [])
+    for kk in range(size_here - 1):
+        if kk % 2 == 0:
+            then.append(
+                jax.lax.ppermute(then[-1] if then else x0, axis_name=axis_name, perm=arrivals)
+            )
+        else:
+            raw_out.append(
+                jax.lax.ppermute(raw_out[-1] if raw_out else x0, axis_name=axis_name, perm=ledger)
+            )
+    val = jnp.stack([*then[::-1], x0, *raw_out], 0)
+    fresh = jax.lax.axis_index(axis_name)
+    mat_out = fresh - len(then)
+    val = val[(jnp.arange(size_here) - mat_out) % size_here]
+    return trace_the_body(val, dim_at)
+
+
+use_map_on_mesh = functools.partial(_perform_panels, axis_name="mp", dim_at=1)
 
 
 def shifted(value, axis, steps):
@@ -118,7 +149,7 @@
     width = stream.shape[1]
     group_at = lax.axis_index("group")
     model_at = lax.axis_index("mp")
-    whole = lax.all_gather(stream, "mp", axis=1, tiled=True)
+    whole = use_map_on_mesh(stream)
     wide = whole.astype(jnp.float32)
     normalized_input = (
         wide * lax.rsqrt(jnp.mean(wide * wide, axis=1, keepdims=True) + 1e-06) * prenorm_gain

time: 255 us -> 231 us (0.906)
  waiting for transfers between devices: 104 us -> 54.1 us
  local copies, waits for them, and re-layouts: 21.9 us -> 37.7 us
  starting transfers between devices: 7.77 us -> 15 us
    all_gather x1, waiting for transfers between devices: 35.3 us -> 0.01 us  [on_device(): lax.all_gather(cached_rotated_keys, 'group', axis=0, tiled=True)]
    all_gather x1 -> x0, waiting for transfers between devices: 28.5 us -> none  [on_device(): whole = lax.all_gather(stream, 'mp', axis=1, tiled=True)]
    ppermute x0 -> x7, waiting for transfers between devices: none -> 18.5 us  [the longest x4 18.5 us: _perform_panels(): jax.lax.ppermute(then[-1] if then else x0, axis_name=axis_name, perm=arri...]
    unnamed x27 -> x36, local copies, waits for them, and re-layouts: 5.37 us -> 16.3 us
    ppermute x0 -> x7, starting transfers between devices: none -> 8.9 us  [the longest x3 8.87 us: _perform_panels(): jax.lax.ppermute(raw_out[-1] if raw_out else x0, axis_name=axis_name, per...]
    gather x0 -> x1, local copies, waits for them, and re-layouts: none -> 4.75 us  [_perform_panels(): val = val[(jnp.arange(size_here) - mat_out) % size_here]]
  transfers between devices with their start and end apart: 7 -> 13, of which waited for: 4 -> 4; matrix products, arithmetic and copies ran while one was open for 22% -> 32% of each run, Pallas kernels for 0% -> 0%
where the time goes in v1:
time: 231 us; the launch traced here: 230 us
  waiting for transfers between devices  54.1 us (23%)
  blocking collectives  52.9 us (23%)
  local copies, waits for them, and re-layouts  37.7 us (16%)
  matrix products  34.2 us (15%)
  other arithmetic  19.7 us (9%)
  between operations  15.9 us (7%)
  starting transfers between devices  15 us (6%)
    reduce_scatter x1, waiting for transfers between devices, on_device(): lax.psum_scatter(partial_out.astype(jnp.bfloat16), 'mp', scatter_dimensio...  34.2 us
    all_gather x1, blocking collectives, on_device(): lax.all_gather(adapter_down_rows, 'group', axis=0, tiled=True)  27.6 us
    psum x1, blocking collectives, on_device(): low = lax.psum(partial_low, 'mp').astype(jnp.bfloat16)  25.3 us
    ppermute x4, waiting for transfers between devices, _perform_panels(): jax.lax.ppermute(then[-1] if then else x0, axis_name=axis_name, perm=arri...  18.5 us
    unnamed x36, local copies, waits for them, and re-layouts  16.3 us
    ppermute x3, starting transfers between devices, _perform_panels(): jax.lax.ppermute(raw_out[-1] if raw_out else x0, axis_name=axis_name, per...  8.87 us
    ppermute x2, starting transfers between devices, shifted(): lax.ppermute(value, axis, [(source, source + steps) for source in range(f...  5.99 us
    dot_general x1, matrix products, on_device(): jnp.dot(normalized_input, query_weight, preferred_element_type=jnp.float32)  5.41 us
  transfers between devices with their start and end apart: 13, of which 4 were waited for; matrix products, arithmetic and copies ran while one was open for 32% of the time, Pallas kernels for 0%

profile of v1, /device:TPU:0, one launch (start us, length us, event | category | flops | bytes accessed | tf_op | source)
XLA Modules:
  0.0 229.6 jit_solution(16639754433139359199)
XLA Ops:
  8.1 2.9 %collective-permute-start.4 = (bf16[512,448]{0,1:T(8,128)(2,1)}, bf16[512,448]{0,1:T(8,128)(2,1)}, u32[]{:S(2)}, u32[]{:S(2)}) collective-permute-start(bf16[512,448]{0,1:T(8,128)(2,1)} %param.16), channel_id=1, source_target_pairs={{1,0},{2,1},{3,2},{4,3},{5,4},{6,5},{7,6},{0,7},{9,8},{10,9},{11,1... | collective-permute-start | bytes 1376264 | tf_op jit(solution)/shard_map/ppermute | solution.py:30
  19.8 27.6 %all_gather.14 = bf16[64,16,448]{2,1,0:T(8,128)(2,1)S(1)} all-gather(bf16[4,16,448]{2,1,0:T(8,128)(2,1)} %param.22), channel_id=1, replica_groups=mesh['group'=16,'mp'=8] {'group'}, dimensions={0}, use_global_device_ids=true | all-gather | bytes 974848 | tf_op jit(solution)/shard_map/all_gather | solution.py:166
  49.5 2.5 %compare_select_fusion.1 = s32[1024,1]{0,1:T(1,128)S(1)} fusion(s32[]{:T(128)} %bitcast.18, s32[]{:T(128)} %bitcast.19, s32[]{:T(128)} %bitcast.21, s32[]{:T(128)} %bitcast.20), kind=kLoop, calls=%fused_computation.79 | loop fusion | flops 17408 | bytes 4112 | tf_op jit(solution)/shard_map/gather | solution.py:106
  54.7 8.6 %collective-permute-done.1 = bf16[512,448]{0,1:T(8,128)(2,1)} collective-permute-done((bf16[512,448]{0,1:T(8,128)(2,1)}, bf16[512,448]{0,1:T(8,128)(2,1)}, u32[]{:S(2)}, u32[]{:S(2)}) %collective-permute-start.1) | collective-permute-done | bytes 458784 | tf_op jit(solution)/shard_map/ppermute | solution.py:26
  64.8 3.0 %collective-permute-start.5 = (bf16[512,448]{0,1:T(8,128)(2,1)}, bf16[512,448]{0,1:T(8,128)(2,1)S(1)}, u32[]{:S(2)}, u32[]{:S(2)}) collective-permute-start(bf16[512,448]{0,1:T(8,128)(2,1)} %collective-permute-done.4), channel_id=1, source_target_pairs={{1,0},{2,1},{3,2},{4,3},{5,4},{6,5},{7,6},{0,7},{9,8},{10,9},{11,1... | collective-permute-start | bytes 1376264 | tf_op jit(solution)/shard_map/ppermute | solution.py:30
  67.7 5.0 %collective-permute-done.2 = bf16[512,448]{0,1:T(8,128)(2,1)} collective-permute-done((bf16[512,448]{0,1:T(8,128)(2,1)}, bf16[512,448]{0,1:T(8,128)(2,1)}, u32[]{:S(2)}, u32[]{:S(2)}) %collective-permute-start.2) | collective-permute-done | bytes 458784 | tf_op jit(solution)/shard_map/ppermute | solution.py:26
  74.2 3.0 %collective-permute-start.6 = (bf16[512,448]{0,1:T(8,128)(2,1)S(1)}, bf16[512,448]{0,1:T(8,128)(2,1)S(1)}, u32[]{:S(2)}, u32[]{:S(2)}) collective-permute-start(bf16[512,448]{0,1:T(8,128)(2,1)S(1)} %collective-permute-done.5), channel_id=1, source_target_pairs={{1,0},{2,1},{3,2},{4,3},{5,4},{6,5},{7,6},{0,7},{9,8},{10,9},{11,1... | collective-permute-start | bytes 1376264 | tf_op jit(solution)/shard_map/ppermute | solution.py:30
  77.2 4.9 %collective-permute-done.3 = bf16[512,448]{0,1:T(8,128)(2,1)S(1)} collective-permute-done((bf16[512,448]{0,1:T(8,128)(2,1)}, bf16[512,448]{0,1:T(8,128)(2,1)S(1)}, u32[]{:S(2)}, u32[]{:S(2)}) %collective-permute-start.3) | collective-permute-done | bytes 458784 | tf_op jit(solution)/shard_map/ppermute | solution.py:26
  93.8 4.7 %gather_fusion = bf16[8,512,448]{1,2,0:T(8,128)(2,1)} fusion(bf16[8,512,448]{1,2,0:T(8,128)(2,1)} %bitcast_dynamic-update-slice_fusion, s32[1024]{0:T(1024)S(1)} %pad_clamp_fusion.1), kind=kCustom, calls=%fused_computation | custom fusion | bytes 7340064 | tf_op jit(solution)/shard_map/gather | solution.py:35
  98.5 3.1 %multiply_reduce_fusion = f32[512]{0:T(512)S(1)} fusion(bf16[8,512,448]{1,2,0:T(8,128)(2,1)} %gather_fusion), kind=kLoop, calls=%fused_computation.9 | loop fusion | flops 5504512 | bytes 3672064 | tf_op jit(solution)/shard_map/reduce_sum | solution.py:155
  108.9 3.1 %collective-permute-start.7 = (bf16[512,256]{1,0:T(8,128)(2,1)}, bf16[512,256]{1,0:T(8,128)(2,1)}, u32[]{:S(2)}, u32[]{:S(2)}) collective-permute-start(bf16[512,256]{1,0:T(8,128)(2,1)} %convolution_convert_fusion.1), channel_id=1, source_target_pairs={{0,8},{8,16},{16,24},{24,32},{32,40},{40,48},{48,56},{56,64},{64,7... | collective-permute-start | bytes 786440 | tf_op jit(solution)/shard_map/ppermute | solution.py:45
  112.0 3.8 %convolution_bitcast_fusion = f32[512,1,256]{0,2,1:T(8,128)S(1)} fusion(bf16[512,3584]{0,1:T(8,128)(2,1)} %copy-done.2, bf16[3584,256]{1,0:T(8,128)(2,1)} %param.19), kind=kOutput, calls=%fused_computation.26 | convolution fusion | flops 939524096 | bytes 6029312 | tf_op jit(solution)/shard_map/dot_general | solution.py:192
  119.5 2.9 %collective-permute-start.8 = (bf16[512,256]{0,1:T(8,128)(2,1)}, bf16[512,256]{0,1:T(8,128)(2,1)}, u32[]{:S(2)}, u32[]{:S(2)}) collective-permute-start(bf16[512,256]{0,1:T(8,128)(2,1)} %maximum_bitcast_fusion.6), channel_id=1, source_target_pairs={{0,8},{8,16},{16,24},{24,32},{32,40},{40,48},{48,56},{56,64},{64,7... | collective-permute-start | bytes 786440 | tf_op jit(solution)/shard_map/ppermute | solution.py:45
  123.5 25.3 %all-reduce.1 = bf16[512,64]{0,1:T(8,128)(2,1)S(1)} all-reduce(f32[512,64]{0,1:T(8,128)S(1)} %bitcast.127), channel_id=1, replica_groups=mesh['group'=16,'mp'=8] {'mp'}, use_global_device_ids=true, to_apply=%region_5.6 | all-reduce | flops 32768 | bytes 196608 | tf_op jit(solution)/shard_map/psum | solution.py:179
  149.0 2.5 %convolution_convert_fusion.2 = bf16[4,16,512]{2,0,1:T(4,128)(2,1)S(1)} fusion(bf16[64,16,512]{2,1,0:T(8,128)(2,1)} %all-gather.8.cloned.1.call-done, s32[4]{0:T(128)S(1)} %gather_fusion.1), kind=kOutput, calls=%fused_computation.28 | convolution fusion | flops 4227328 | bytes 1114128 | tf_op jit(solution)/shard_map/rj,jkd->rkd/dot_general | solution.py:172
  151.8 5.4 %convolution_add_fusion = f32[512,512]{0,1:T(8,128)S(1)} fusion(f32[512,512]{0,1:T(8,128)S(1)} %convolution_multiply_fusion, bf16[512,3584]{0,1:T(8,128)(2,1)} %copy-done.2, bf16[3584,512]{1,0:T(8,128)(2,1)} %param.18), kind=kOutput, calls=%fused_computation.23 | convolution fusion | flops 1879310336 | bytes 9437184 | tf_op jit(solution)/shard_map/dot_general | solution.py:187
  159.6 2.1 copy.62
  161.7 2.1 subtract_convert_fusion
  167.4 4.6 %fusion.16 = bf16[4,256,256]{2,0,1:T(4,128)(2,1)S(1)} fusion(bf16[32,256,256]{2,1,0:T(8,128)(2,1)} %all-gather.4.cloned.1.call-done, s32[4]{0:T(128)S(1)} %dynamic-slice_reduce_fusion.1), kind=kOutput, calls=%fused_computation.24 | convolution fusion | flops 17039488 | bytes 4718608 | tf_op jit(solution)/shard_map/rj,jcd->rcd/dot_general | solution.py:208
  173.2 4.7 %fusion.19 = bf16[4,256,256]{2,0,1:T(4,128)(2,1)S(1)} fusion(bf16[32,256,256]{2,1,0:T(8,128)(2,1)} %all-gather.6.cloned.1.call-done, s32[4]{0:T(128)S(1)} %dynamic-slice_reduce_fusion.1), kind=kOutput, calls=%fused_computation.25 | convolution fusion | flops 17039488 | bytes 4718608 | tf_op jit(solution)/shard_map/rj,jcd->rcd/dot_general | solution.py:207
  179.9 2.2 fusion
  182.1 2.8 %divide_convert_fusion = bf16[512,1,2,256]{0,3,2,1:T(8,128)(2,1)S(1)} fusion(f32[2048,512,2]{1,0,2:T(8,128)S(1)} %get-tuple-element.25, f32[2,512]{1,0:T(2,128)S(1)} %get-tuple-element.24, pred[512,2048]{0,1:T(8,128)(4,1)S(1)} %pad_add_fusion, bf16[512,256]{0,1:T(8,128)(2,1)S(1)} %copy-done.4, bf16[512,256]{0,1:T(8,128)(2,1)S(1)} %copy-done.6, ...), kind=kOutput, calls=%fused_computation.43 | convolution fusion | flops 1085800448 | bytes 11018240 | tf_op jit(solution)/shard_map/krts,skd->tkrd/dot_general | solution.py:120
  185.0 3.9 %convolution_convert_fusion = bf16[512,3584]{0,1:T(8,128)(2,1)} fusion(bf16[512,512]{0,1:T(8,128)(2,1)S(1)} %bitcast.133, bf16[512,3584]{1,0:T(8,128)(2,1)S(1)} %copy-done.12), kind=kOutput, calls=%fused_computation.11 | convolution fusion | flops 1880883200 | bytes 7864320 | tf_op jit(solution)/shard_map/dot_general | solution.py:225
  188.9 34.2 %reduce-scatter.2.cloned.1.call-done = bf16[512,448]{0,1:T(8,128)(2,1)} async-done(((bf16[512,3584]{0,1:T(8,128)(2,1)}), bf16[512,448]{0,1:T(8,128)(2,1)}) %reduce-scatter.2.cloned.1.call-update) | async-done | bytes 458768 | tf_op jit(solution)/shard_map/reduce_scatter | solution.py:226
  (102 shorter events, 48.8 us)
Async XLA Ops:
  6.5 98.7 %copy-start = (bf16[3584,256]{1,0:T(8,128)(2,1)S(1)}, bf16[3584,256]{1,0:T(8,128)(2,1)}, u32[]{:S(2)}) copy-start(bf16[3584,256]{1,0:T(8,128)(2,1)} %param.20) | copy-start | bytes 5505028
  6.5 58.0 %copy-start.11 = (s32[16,4]{0,1:T(4,128)S(1)}, s32[16,4]{0,1:T(4,128)}, u32[]{:S(2)}) copy-start(s32[16,4]{0,1:T(4,128)} %param.28) | copy-start | bytes 772
  6.5 142.4 %all-gather.8.cloned.1.call-start = ((), (), s32[]{:S(2)}) async-start(), calls=%async_computation.3 | async-start | bytes 1114112 | tf_op jit(solution)/shard_map/all_gather | solution.py:167
  7.3 160.2 %all-gather.4.cloned.1.call-start = ((), (), s32[]{:S(2)}) async-start(), calls=%async_computation.1 | async-start | bytes 4456448 | tf_op jit(solution)/shard_map/all_gather | solution.py:203
  8.0 165.1 %all-gather.6.cloned.1.call-start = ((), (), s32[]{:S(2)}) async-start(), calls=%async_computation.2 | async-start | bytes 4456448 | tf_op jit(solution)/shard_map/all_gather | solution.py:202
  8.1 45.8 %collective-permute-start = (bf16[512,448]{0,1:T(8,128)(2,1)}, bf16[512,448]{0,1:T(8,128)(2,1)}, u32[]{:S(2)}, u32[]{:S(2)}) collective-permute-start(bf16[512,448]{0,1:T(8,128)(2,1)} %param.16), channel_id=1, source_target_pairs={{0,1},{1,2},{2,3},{3,4},{4,5},{5,6},{6,7},{7,0},{8,9},{9,10},{10,1... | collective-permute-start | bytes 1376264 | tf_op jit(solution)/shard_map/ppermute | solution.py:26
  8.1 56.7 %collective-permute-start.4 = (bf16[512,448]{0,1:T(8,128)(2,1)}, bf16[512,448]{0,1:T(8,128)(2,1)}, u32[]{:S(2)}, u32[]{:S(2)}) collective-permute-start(bf16[512,448]{0,1:T(8,128)(2,1)} %param.16), channel_id=1, source_target_pairs={{1,0},{2,1},{3,2},{4,3},{5,4},{6,5},{7,6},{0,7},{9,8},{10,9},{11,1... | collective-permute-start | bytes 1376264 | tf_op jit(solution)/shard_map/ppermute | solution.py:30
  11.0 212.0 %reduce-scatter.2.cloned.1.call-start = ((), (), s32[]{:S(2)}) async-start(), calls=%async_computation.4 | async-start | bytes 4128768 | tf_op jit(solution)/shard_map/reduce_scatter | solution.py:226
  53.9 9.4 %collective-permute-start.1 = (bf16[512,448]{0,1:T(8,128)(2,1)}, bf16[512,448]{0,1:T(8,128)(2,1)}, u32[]{:S(2)}, u32[]{:S(2)}) collective-permute-start(bf16[512,448]{0,1:T(8,128)(2,1)} %collective-permute-done), channel_id=1, source_target_pairs={{0,1},{1,2},{2,3},{3,4},{4,5},{5,6},{6,7},{7,0},{8,9},{9,10},{10,1... | collective-permute-start | bytes 1376264 | tf_op jit(solution)/shard_map/ppermute | solution.py:26
  63.3 9.4 %collective-permute-start.2 = (bf16[512,448]{0,1:T(8,128)(2,1)}, bf16[512,448]{0,1:T(8,128)(2,1)}, u32[]{:S(2)}, u32[]{:S(2)}) collective-permute-start(bf16[512,448]{0,1:T(8,128)(2,1)} %collective-permute-done.1), channel_id=1, source_target_pairs={{0,1},{1,2},{2,3},{3,4},{4,5},{5,6},{6,7},{7,0},{8,9},{9,10},{10,1... | collective-permute-start | bytes 1376264 | tf_op jit(solution)/shard_map/ppermute | solution.py:26
  64.8 9.5 %collective-permute-start.5 = (bf16[512,448]{0,1:T(8,128)(2,1)}, bf16[512,448]{0,1:T(8,128)(2,1)S(1)}, u32[]{:S(2)}, u32[]{:S(2)}) collective-permute-start(bf16[512,448]{0,1:T(8,128)(2,1)} %collective-permute-done.4), channel_id=1, source_target_pairs={{1,0},{2,1},{3,2},{4,3},{5,4},{6,5},{7,6},{0,7},{9,8},{10,9},{11,1... | collective-permute-start | bytes 1376264 | tf_op jit(solution)/shard_map/ppermute | solution.py:30
  72.7 9.3 %collective-permute-start.3 = (bf16[512,448]{0,1:T(8,128)(2,1)}, bf16[512,448]{0,1:T(8,128)(2,1)S(1)}, u32[]{:S(2)}, u32[]{:S(2)}) collective-permute-start(bf16[512,448]{0,1:T(8,128)(2,1)} %collective-permute-done.2), channel_id=1, source_target_pairs={{0,1},{1,2},{2,3},{3,4},{4,5},{5,6},{6,7},{7,0},{8,9},{9,10},{10,1... | collective-permute-start | bytes 1376264 | tf_op jit(solution)/shard_map/ppermute | solution.py:26
  74.2 18.7 %collective-permute-start.6 = (bf16[512,448]{0,1:T(8,128)(2,1)S(1)}, bf16[512,448]{0,1:T(8,128)(2,1)S(1)}, u32[]{:S(2)}, u32[]{:S(2)}) collective-permute-start(bf16[512,448]{0,1:T(8,128)(2,1)S(1)} %collective-permute-done.5), channel_id=1, source_target_pairs={{1,0},{2,1},{3,2},{4,3},{5,4},{6,5},{7,6},{0,7},{9,8},{10,9},{11,1... | collective-permute-start | bytes 1376264 | tf_op jit(solution)/shard_map/ppermute | solution.py:30
  93.8 7.9 %copy-start.10 = (f32[3584]{0:T(1024)S(1)}, f32[3584]{0:T(1024)}, u32[]{:S(2)}) copy-start(f32[3584]{0:T(1024)} %param.17) | copy-start | bytes 43012
  98.5 3.3 %copy-start.1 = (bf16[8,512,448]{1,2,0:T(8,128)(2,1)S(1)}, bf16[8,512,448]{1,2,0:T(8,128)(2,1)}, u32[]{:S(2)}) copy-start(bf16[8,512,448]{1,2,0:T(8,128)(2,1)} %gather_fusion) | copy-start | bytes 11010052
  108.9 54.9 %collective-permute-start.7 = (bf16[512,256]{1,0:T(8,128)(2,1)}, bf16[512,256]{1,0:T(8,128)(2,1)}, u32[]{:S(2)}, u32[]{:S(2)}) collective-permute-start(bf16[512,256]{1,0:T(8,128)(2,1)} %convolution_convert_fusion.1), channel_id=1, source_target_pairs={{0,8},{8,16},{16,24},{24,32},{32,40},{40,48},{48,56},{56,64},{64,7... | collective-permute-start | bytes 786440 | tf_op jit(solution)/shard_map/ppermute | solution.py:45
  119.5 46.1 %collective-permute-start.8 = (bf16[512,256]{0,1:T(8,128)(2,1)}, bf16[512,256]{0,1:T(8,128)(2,1)}, u32[]{:S(2)}, u32[]{:S(2)}) collective-permute-start(bf16[512,256]{0,1:T(8,128)(2,1)} %maximum_bitcast_fusion.6), channel_id=1, source_target_pairs={{0,8},{8,16},{16,24},{24,32},{32,40},{40,48},{48,56},{56,64},{64,7... | collective-permute-start | bytes 786440 | tf_op jit(solution)/shard_map/ppermute | solution.py:45
  173.1 4.8 %copy-start.5 = (bf16[512,256]{1,0:T(8,128)(2,1)S(1)}, bf16[512,256]{1,0:T(8,128)(2,1)}, u32[]{:S(2)}) copy-start(bf16[512,256]{1,0:T(8,128)(2,1)} %copy.52) | copy-start | bytes 786436
  173.1 4.8 %copy-start.7 = (bf16[512,256]{1,0:T(8,128)(2,1)S(1)}, bf16[512,256]{1,0:T(8,128)(2,1)}, u32[]{:S(2)}) copy-start(bf16[512,256]{1,0:T(8,128)(2,1)} %copy.51) | copy-start | bytes 786436
  173.1 4.8 %copy-start.8 = (bf16[512,2,128]{2,0,1:T(8,128)(2,1)S(1)}, bf16[512,2,128]{2,0,1:T(8,128)(2,1)}, u32[]{:S(2)}) copy-start(bf16[512,2,128]{2,0,1:T(8,128)(2,1)} %get-tuple-element.12) | copy-start | bytes 786436
  173.2 4.8 %copy-start.9 = (bf16[512,2,128]{2,0,1:T(8,128)(2,1)S(1)}, bf16[512,2,128]{2,0,1:T(8,128)(2,1)}, u32[]{:S(2)}) copy-start(bf16[512,2,128]{2,0,1:T(8,128)(2,1)} %get-tuple-element.13) | copy-start | bytes 786436
  179.9 2.2 copy-start.3
  179.9 2.2 copy-start.4
  182.1 2.8 %copy-start.12 = (bf16[512,3584]{1,0:T(8,128)(2,1)S(1)}, bf16[512,3584]{1,0:T(8,128)(2,1)}, u32[]{:S(2)}) copy-start(bf16[512,3584]{1,0:T(8,128)(2,1)} %param.21) | copy-start | bytes 11010052
  (2 other events, 4.1 us)
Sparse Core Ops, SparseCore 0:
  9.5 45.5 all-gather.7
  57.2 50.7 all-gather.3
  110.2 52.4 all-gather.5
  189.0 33.9 reduce-scatter.1
